TPU v7x, 32 devices: a whole 2x2x4 slice. The times are simulated.
32 devices in a mesh: grp: 2 (over y), row: 4 (over z), head: 2 (over x), rep: 2 (over core).
Axes of the slice: x: 2, y: 2, z: 4, core: 2. Of those that a mesh axis runs over, the one named last changes fastest.
Arguments:
- queries: float32 [2048, 8192], P(('grp', 'row', 'rep'), 'head'), parts along dimension 0
- key_max: float32 [4096, 1024], P(('grp', 'row', 'rep'), 'head'), parts along dimension 0
- key_min: float32 [4096, 1024], P(('grp', 'row', 'rep'), 'head'), parts along dimension 0, as said below
- limits: int32 [2048], P(('grp', 'row', 'rep')), parts along dimension 0, may hold values from 0 to 2047, as said below
Outputs:
- page_mass: float32 [2048, 2048], P(('grp', 'row', 'rep'), 'head'), parts along dimension 0
There are 2 independent parts, one for each index of `grp`. A program takes and returns all parts, laid end to end along the dimension named above; each array names one. Nothing has to cross between parts.
Inputs may be any that keep to these rules, and one draw needn't show every extreme that they name: key_min <= key_max in every entry. Rows of the i-th aligned block of 128 rows have limits within the i-th block of 256 pages, not falling within a block; the first block's first row has the first page and the last block's last row the last page.
All inputs are finite; a program needn't handle non-finite values.
Results may differ from a plain program's by a relative error of at most 0.00013.
Values sent between devices are 32-bit elements; how exact they have to be, the bound alone decides.
No kernel may reach another device: no remote copies, remote signals or barrier semaphores. Data moves between devices by JAX's collectives and lax.ppermute only.
A program may use at most 64 MiB of HBM per device.

v0:
```python
import math
import jax
import jax.numpy as jnp
from jax import lax
from jax.sharding import PartitionSpec as P

DH = 128


def per_device(queries, key_max, key_min, limits):
    head_count = queries.shape[1] // DH
    kv_count = key_max.shape[1] // DH
    group_size = head_count // kv_count
    score_scale = 1.0 / math.sqrt(DH)
    bounds = jnp.stack((key_max, key_min))
    query_rows, row_limits = (queries, limits)
    gathered = lax.all_gather(bounds, ("row", "rep"), axis=1, tiled=True)
    page_ids = jnp.arange(gathered.shape[1], dtype=jnp.int32)
    row_count = query_rows.shape[0]
    page_count = gathered.shape[1]
    head_rows = query_rows.reshape(row_count, head_count, DH).transpose(1, 0, 2)
    positive = jnp.maximum(head_rows, 0.0)
    negative = jnp.minimum(head_rows, 0.0)
    sheets = gathered.reshape(2, page_count, kv_count, DH).transpose(2, 0, 1, 3)
    visible = page_ids[None, :] <= row_limits[:, None]

    def head_scores(head_index, kv_index):
        upper_part = jnp.dot(
            positive[head_index], sheets[kv_index, 0].T, precision=lax.Precision.HIGHEST
        )
        return upper_part + jnp.dot(
            negative[head_index], sheets[kv_index, 1].T, precision=lax.Precision.HIGHEST
        )

    def head_step(accumulated, head_index):
        raw_scores = head_scores(head_index, head_index // group_size)
        masked = jnp.where(visible, raw_scores * score_scale, -1e30)
        row_top = jnp.max(masked, axis=1, keepdims=True)
        weights = jnp.exp(masked - row_top)
        row_total = jnp.sum(weights, axis=1, keepdims=True)
        return (accumulated + weights / row_total, None)

    start = jnp.zeros((row_count, page_count), jnp.float32)
    accumulated, unused = lax.scan(head_step, start, jnp.arange(head_count, dtype=jnp.int32))
    return lax.psum_scatter(accumulated, "head", scatter_dimension=1, tiled=True)


def solution(mesh):
    placed = (
        P(("grp", "row", "rep"), "head"),
        P(("grp", "row", "rep"), "head"),
        P(("grp", "row", "rep"), "head"),
        P(("grp", "row", "rep")),
    )
    return jax.shard_map(
        per_device,
        mesh=mesh,
        in_specs=placed,
        out_specs=P(("grp", "row", "rep"), "head"),
        check_vma=False,
    )
```

profile of v0, /device:TPU:0, one launch (start us, length us, event | category | flops | bytes accessed | tf_op | source)
XLA Modules:
  0.0 448.6 jit_solution(9973003947528456110)
XLA Ops:
  14.3 80.7 %all-gather.2.cloned.1.call-done = f32[2,2048,512]{1,2,0:T(8,128)} async-done(((f32[2,256,512]{1,2,0:T(8,128)}), f32[2,2048,512]{1,2,0:T(8,128)}) %all-gather.2.cloned.1.call-update) | async-done | bytes 8388624 | tf_op jit(solution)/shard_map/all_gather | solution.py:17
  95.0 8.7 %copy.10 = f32[4,2,2048,128]{3,2,1,0:T(8,128)} copy(f32[4,2,2048,128]{2,3,0,1:T(8,128)} %bitcast.40) | data formatting | bytes 16777216
  103.8 318.0 %while.13 = (s32[]{:T(128)}, f32[128,2048]{1,0:T(8,128)S(1)}, s32[32]{0:T(128)S(1)}, f32[32,128,128]{1,2,0:T(8,128)}, f32[4,2,2048,128]{3,2,1,0:T(8,128)}, /*ind...) while((s32[]{:T(128)}, f32[128,2048]{1,0:T(8,128)S(1)}, ...), condition=%wide.region_3.4_spmd.clone, body=%wide.region_0.3_spmd.clone.sunk | while | flops 808189696 | bytes 9571716 | solution.py:44
  108.1 2.3 fusion.25
  110.4 2.6 fusion.26
  118.0 2.3 fusion.25
  120.4 2.6 fusion.26
  128.0 2.3 fusion.25
  130.3 2.6 fusion.26
  137.9 2.3 fusion.25
  140.3 2.6 fusion.26
  147.9 2.3 fusion.25
  150.2 2.6 fusion.26
  157.8 2.3 fusion.25
  160.1 2.6 fusion.26
  167.7 2.3 fusion.25
  170.1 2.6 fusion.26
  177.7 2.3 fusion.25
  180.0 2.6 fusion.26
  187.6 2.3 fusion.25
  189.9 2.6 fusion.26
  197.5 2.3 fusion.25
  199.9 2.6 fusion.26
  207.5 2.3 fusion.25
  209.8 2.6 fusion.26
  217.4 2.3 fusion.25
  219.7 2.6 fusion.26
  227.4 2.3 fusion.25
  229.7 2.6 fusion.26
  237.3 2.3 fusion.25
  239.6 2.6 fusion.26
  247.2 2.3 fusion.25
  249.6 2.6 fusion.26
  257.2 2.3 fusion.25
  259.5 2.6 fusion.26
  267.1 2.3 fusion.25
  269.4 2.6 fusion.26
  277.0 2.3 fusion.25
  279.4 2.6 fusion.26
  287.0 2.3 fusion.25
  289.3 2.6 fusion.26
  296.9 2.3 fusion.25
  299.2 2.6 fusion.26
  306.8 2.3 fusion.25
  309.2 2.6 fusion.26
  316.8 2.3 fusion.25
  319.1 2.6 fusion.26
  326.7 2.3 fusion.25
  329.1 2.6 fusion.26
  336.7 2.3 fusion.25
  339.0 2.6 fusion.26
  348.9 2.6 fusion.26
  356.5 2.3 fusion.25
  358.9 2.6 fusion.26
  368.8 2.6 fusion.26
  376.4 2.3 fusion.25
  378.7 2.6 fusion.26
  386.3 2.3 fusion.25
  388.7 2.6 fusion.26
  398.6 2.6 fusion.26
  406.2 2.3 fusion.25
  408.5 2.6 fusion.26
  418.5 2.6 fusion.26
  422.7 19.0 %reduce-scatter.2.cloned.1.call-done = f32[128,1024]{1,0:T(8,128)} async-done(((f32[128,2048]{1,0:T(8,128)}), f32[128,1024]{1,0:T(8,128)}) %reduce-scatter.2.cloned.1.call-update) | async-done | bytes 524304 | tf_op jit(solution)/shard_map/reduce_scatter | solution.py:45
  (115 shorter events, 58.2 us)
Async XLA Ops:
  6.5 88.5 %all-gather.2.cloned.1.call-start = ((), (), s32[]{:S(2)}) async-start(), calls=%async_computation.1 | async-start | bytes 9437184 | tf_op jit(solution)/shard_map/all_gather | solution.py:17
  10.1 431.6 %reduce-scatter.2.cloned.1.call-start = ((), (), s32[]{:S(2)}) async-start(), calls=%async_computation.2 | async-start | bytes 1572864 | tf_op jit(solution)/shard_map/reduce_scatter | solution.py:45
  95.0 8.8 %copy-start.1 = (s32[128]{0:T(128)S(1)}, s32[128]{0:T(128)}, u32[]{:S(2)}) copy-start(s32[128]{0:T(128)} %param.9) | copy-start | bytes 1540
  421.7 1.0 copy-start
Sparse Core Ops, SparseCore 0:
  10.2 84.7 all-gather.1
  422.9 18.8 reduce-scatter.1
where the time goes:
time: 452 us; the launch traced here: 449 us
  matrix products  157 us (35%)
  loops' own time  121 us (27%)
  waiting for transfers between devices  99.8 us (22%)
  local copies, waits for them, and re-layouts  33.2 us (7%)
  other arithmetic  24.4 us (5%)
  between operations  13.4 us (3%)
    another operation x1, loops' own time, per_device(): lax.scan(head_step, start, jnp.arange(head_count, dtype=jnp.int32))  121 us
    dot_general x32, matrix products, head_scores(): jnp.dot(negative[head_index], sheets[kv_index, 1].T, precision=lax.Precis...  82.2 us
    all_gather x1, waiting for transfers between devices, per_device(): gathered = lax.all_gather(bounds, ('row', 'rep'), axis=1, tiled=True)  80.7 us
    dot_general x32, matrix products, head_scores(): jnp.dot(positive[head_index], sheets[kv_index, 0].T, precision=lax.Precis...  74.5 us
    dynamic_slice x32, local copies, waits for them, and re-layouts, per_device(): lax.scan(head_step, start, jnp.arange(head_count, dtype=jnp.int32))  19.1 us
    reduce_scatter x1, waiting for transfers between devices, per_device(): lax.psum_scatter(accumulated, 'head', scatter_dimension=1, tiled=True)  19 us
    unnamed x8, local copies, waits for them, and re-layouts  14.1 us
    add x32, other arithmetic, head_step(): return (accumulated + weights / row_total, None)  11.5 us
  transfers between devices with their start and end apart: 2, of which 2 were waited for; matrix products, arithmetic and copies ran while one was open for 1% of the time, Pallas kernels for 0%

commit v1 on v0

--- a/solution.py
+++ b/solution.py
@@ -7,6 +7,19 @@
 DH = 128
 
 
+def gather_around(value, axis, dim):
+    ways = lax.axis_size(axis)
+    up = [(d, (d + 1) % ways) for d in range(ways)]
+    down = [(d, (d - 1) % ways) for d in range(ways)]
+    earlier, later = ([value], [value])
+    for _ in range(ways // 2):
+        earlier.append(lax.ppermute(earlier[-1], axis, up))
+    for _ in range((ways - 1) // 2):
+        later.append(lax.ppermute(later[-1], axis, down))
+    line = jnp.concatenate([*earlier[::-1], *later[1:]], axis=dim)
+    return jnp.roll(line, (lax.axis_index(axis) - ways // 2) * value.shape[dim], axis=dim)
+
+
 def per_device(queries, key_max, key_min, limits):
     head_count = queries.shape[1] // DH
     kv_count = key_max.shape[1] // DH
@@ -14,7 +27,7 @@
     score_scale = 1.0 / math.sqrt(DH)
     bounds = jnp.stack((key_max, key_min))
     query_rows, row_limits = (queries, limits)
-    gathered = lax.all_gather(bounds, ("row", "rep"), axis=1, tiled=True)
+    gathered = gather_around(bounds, ("row", "rep"), 1)
     page_ids = jnp.arange(gathered.shape[1], dtype=jnp.int32)
     row_count = query_rows.shape[0]
     page_count = gathered.shape[1]

time: 452 us -> 490 us (1.084)
  local copies, waits for them, and re-layouts: 33.2 us -> 54.5 us
  starting transfers between devices: 0.04 us -> 12.1 us
  loops' own time: 121 us -> 126 us
    all_gather x1 -> x0, waiting for transfers between devices: 80.7 us -> none  [per_device(): gathered = lax.all_gather(bounds, ('row', 'rep'), axis=1, tiled=True)]
    ppermute x0 -> x7, waiting for transfers between devices: none -> 71.7 us  [the longest x4 71.2 us: gather_around(): earlier.append(lax.ppermute(earlier[-1], axis, up))]
    unnamed x8 -> x33, local copies, waits for them, and re-layouts: 14.1 us -> 30.6 us
    ppermute x0 -> x7, starting transfers between devices: none -> 12.1 us  [the longest x3 11.6 us: gather_around(): later.append(lax.ppermute(later[-1], axis, down))]
    reduce_scatter x1, waiting for transfers between devices: 19 us -> 27 us  [per_device(): lax.psum_scatter(accumulated, 'head', scatter_dimension=1, tiled=True)]
  transfers between devices with their start and end apart: 2 -> 8, of which waited for: 2 -> 6; matrix products, arithmetic and copies ran while one was open for 1% -> 3% of each run, Pallas kernels for 0% -> 0%
where the time goes in v1:
time: 490 us; the launch traced here: 486 us
  matrix products  156 us (32%)
  loops' own time  126 us (26%)
  waiting for transfers between devices  98.7 us (20%)
  local copies, waits for them, and re-layouts  54.5 us (11%)
  other arithmetic  24.4 us (5%)
  between operations  13.7 us (3%)
  starting transfers between devices  12.1 us (2%)
    another operation x1, loops' own time, per_device(): lax.scan(head_step, start, jnp.arange(head_count, dtype=jnp.int32))  126 us
    dot_general x32, matrix products, head_scores(): jnp.dot(negative[head_index], sheets[kv_index, 1].T, precision=lax.Precis...  81.8 us
    dot_general x32, matrix products, head_scores(): jnp.dot(positive[head_index], sheets[kv_index, 0].T, precision=lax.Precis...  74.4 us
    ppermute x4, waiting for transfers between devices, gather_around(): earlier.append(lax.ppermute(earlier[-1], axis, up))  71.2 us
    unnamed x33, local copies, waits for them, and re-layouts  30.6 us
    reduce_scatter x1, waiting for transfers between devices, per_device(): lax.psum_scatter(accumulated, 'head', scatter_dimension=1, tiled=True)  27 us
    dynamic_slice x32, local copies, waits for them, and re-layouts, per_device(): lax.scan(head_step, start, jnp.arange(head_count, dtype=jnp.int32))  18.8 us
    ppermute x3, starting transfers between devices, gather_around(): later.append(lax.ppermute(later[-1], axis, down))  11.6 us
  transfers between devices with their start and end apart: 8, of which 6 were waited for; matrix products, arithmetic and copies ran while one was open for 3% of the time, Pallas kernels for 0%

profile of v1, /device:TPU:0, one launch (start us, length us, event | category | flops | bytes accessed | tf_op | source)
XLA Modules:
  0.0 485.6 jit_solution(18415792158599512535)
XLA Ops:
  9.8 4.1 collective-permute-start.4
  13.9 21.0 %collective-permute-done = f32[2,256,512]{1,2,0:T(8,128)S(1)} collective-permute-done((f32[2,256,512]{1,2,0:T(8,128)S(1)}, f32[2,256,512]{1,2,0:T(8,128)S(1)}, u32[]{:S(2)}, u32[]{:S(2)}) %collective-permute-start) | collective-permute-done | bytes 1048608 | tf_op jit(solution)/shard_map/ppermute | solution.py:16
  35.4 3.9 collective-permute-start.5
  39.3 19.2 %collective-permute-done.1 = f32[2,256,512]{1,2,0:T(8,128)} collective-permute-done((f32[2,256,512]{1,2,0:T(8,128)S(1)}, f32[2,256,512]{1,2,0:T(8,128)}, u32[]{:S(2)}, u32[]{:S(2)}) %collective-permute-start.1) | collective-permute-done | bytes 1048608 | tf_op jit(solution)/shard_map/ppermute | solution.py:16
  60.5 3.6 collective-permute-start.6
  64.1 14.6 %collective-permute-done.2 = f32[2,256,512]{1,2,0:T(8,128)} collective-permute-done((f32[2,256,512]{1,2,0:T(8,128)}, f32[2,256,512]{1,2,0:T(8,128)}, u32[]{:S(2)}, u32[]{:S(2)}) %collective-permute-start.2) | collective-permute-done | bytes 1048608 | tf_op jit(solution)/shard_map/ppermute | solution.py:16
  80.9 16.5 %collective-permute-done.3 = f32[2,256,512]{1,2,0:T(8,128)} collective-permute-done((f32[2,256,512]{1,2,0:T(8,128)}, f32[2,256,512]{1,2,0:T(8,128)}, u32[]{:S(2)}, u32[]{:S(2)}) %collective-permute-start.3) | collective-permute-done | bytes 1048608 | tf_op jit(solution)/shard_map/ppermute | solution.py:16
  116.7 3.8 constant_dynamic-slice_fusion
  120.5 8.7 %copy.10 = f32[4,2,2048,128]{3,2,1,0:T(8,128)} copy(f32[4,2,2048,128]{2,3,0,1:T(8,128)} %bitcast.40) | data formatting | bytes 16777216
  129.2 321.5 %while.13 = (s32[]{:T(128)}, f32[128,2048]{1,0:T(8,128)S(1)}, s32[32]{0:T(128)S(1)}, f32[32,128,128]{1,2,0:T(8,128)}, f32[4,2,2048,128]{3,2,1,0:T(8,128)}, /*ind...) while((s32[]{:T(128)}, f32[128,2048]{1,0:T(8,128)S(1)}, ...), condition=%wide.region_3.4_spmd.clone, body=%wide.region_0.3_spmd.clone.sunk | while | flops 808189696 | bytes 9571708 | solution.py:57
  133.7 2.3 fusion.25
  136.0 2.6 fusion.26
  143.8 2.3 fusion.25
  146.1 2.6 fusion.26
  156.1 2.6 fusion.26
  163.9 2.3 fusion.25
  166.2 2.6 fusion.26
  173.9 2.3 fusion.25
  176.2 2.6 fusion.26
  184.0 2.3 fusion.25
  186.3 2.6 fusion.26
  196.3 2.6 fusion.26
  204.0 2.3 fusion.25
  206.4 2.6 fusion.26
  214.1 2.3 fusion.25
  216.4 2.6 fusion.26
  224.1 2.3 fusion.25
  226.5 2.6 fusion.26
  236.5 2.6 fusion.26
  244.2 2.3 fusion.25
  246.6 2.6 fusion.26
  254.3 2.3 fusion.25
  256.6 2.6 fusion.26
  264.3 2.3 fusion.25
  266.7 2.6 fusion.26
  276.7 2.6 fusion.26
  284.4 2.3 fusion.25
  286.8 2.6 fusion.26
  294.5 2.3 fusion.25
  296.8 2.6 fusion.26
  304.5 2.3 fusion.25
  306.9 2.6 fusion.26
  316.9 2.6 fusion.26
  324.6 2.3 fusion.25
  327.0 2.6 fusion.26
  334.7 2.3 fusion.25
  337.0 2.6 fusion.26
  344.7 2.3 fusion.25
  347.1 2.6 fusion.26
  357.1 2.6 fusion.26
  364.8 2.3 fusion.25
  367.2 2.6 fusion.26
  374.9 2.3 fusion.25
  377.2 2.6 fusion.26
  384.9 2.3 fusion.25
  387.3 2.6 fusion.26
  397.3 2.6 fusion.26
  407.3 2.6 fusion.26
  415.1 2.3 fusion.25
  417.4 2.6 fusion.26
  427.4 2.6 fusion.26
  437.5 2.6 fusion.26
  447.5 2.6 fusion.26
  451.8 27.0 %reduce-scatter.2.cloned.1.call-done = f32[128,1024]{1,0:T(8,128)} async-done(((f32[128,2048]{1,0:T(8,128)}), f32[128,1024]{1,0:T(8,128)}) %reduce-scatter.2.cloned.1.call-update) | async-done | bytes 524304 | tf_op jit(solution)/shard_map/reduce_scatter | solution.py:58
  (155 shorter events, 93.0 us)
Async XLA Ops:
  6.5 472.2 %reduce-scatter.2.cloned.1.call-start = ((), (), s32[]{:S(2)}) async-start(), calls=%async_computation.1 | async-start | bytes 1572864 | tf_op jit(solution)/shard_map/reduce_scatter | solution.py:58
  7.8 73.1 %copy-start.1 = (f32[256,512]{0,1:T(8,128)}, f32[256,512]{0,1:T(8,128)S(1)}, u32[]{:S(2)}) copy-start(f32[256,512]{0,1:T(8,128)S(1)} %copy.6) | copy-start | bytes 1572868
  9.2 71.7 %copy-start.3 = (f32[256,512]{0,1:T(8,128)}, f32[256,512]{0,1:T(8,128)S(1)}, u32[]{:S(2)}) copy-start(f32[256,512]{0,1:T(8,128)S(1)} %copy.7) | copy-start | bytes 1572868
  9.3 25.6 %collective-permute-start = (f32[2,256,512]{1,2,0:T(8,128)S(1)}, f32[2,256,512]{1,2,0:T(8,128)S(1)}, u32[]{:S(2)}, u32[]{:S(2)}) collective-permute-start(f32[2,256,512]{1,2,0:T(8,128)S(1)} %pad_maximum_fusion), channel_id=1, source_target_pairs={{0,1},{1,4},{4,5},{5,8},{8,9},{9,12},{12,13},{13,0},{2,3},{3,6},{6... | collective-permute-start | bytes 3145736 | tf_op jit(solution)/shard_map/ppermute | solution.py:16
  9.8 25.6 %collective-permute-start.4 = (f32[2,256,512]{1,2,0:T(8,128)S(1)}, f32[2,256,512]{1,2,0:T(8,128)}, u32[]{:S(2)}, u32[]{:S(2)}) collective-permute-start(f32[2,256,512]{1,2,0:T(8,128)S(1)} %pad_maximum_fusion), channel_id=1, source_target_pairs={{0,13},{1,0},{4,1},{5,4},{8,5},{9,8},{12,9},{13,12},{2,15},{3,2},{... | collective-permute-start | bytes 3145736 | tf_op jit(solution)/shard_map/ppermute | solution.py:18
  34.9 23.6 %copy-start.5 = (f32[2,256,512]{1,2,0:T(8,128)}, f32[2,256,512]{1,2,0:T(8,128)S(1)}, u32[]{:S(2)}) copy-start(f32[2,256,512]{1,2,0:T(8,128)S(1)} %collective-permute-done) | copy-start | bytes 3145732
  34.9 23.6 %collective-permute-start.1 = (f32[2,256,512]{1,2,0:T(8,128)S(1)}, f32[2,256,512]{1,2,0:T(8,128)}, u32[]{:S(2)}, u32[]{:S(2)}) collective-permute-start(f32[2,256,512]{1,2,0:T(8,128)S(1)} %collective-permute-done), channel_id=1, source_target_pairs={{0,1},{1,4},{4,5},{5,8},{8,9},{9,12},{12,13},{13,0},{2,3},{3,6},{6... | collective-permute-start | bytes 3145736 | tf_op jit(solution)/shard_map/ppermute | solution.py:16
  35.4 25.0 %collective-permute-start.5 = (f32[2,256,512]{1,2,0:T(8,128)}, f32[2,256,512]{1,2,0:T(8,128)}, u32[]{:S(2)}, u32[]{:S(2)}) collective-permute-start(f32[2,256,512]{1,2,0:T(8,128)} %collective-permute-done.4), channel_id=1, source_target_pairs={{0,13},{1,0},{4,1},{5,4},{8,5},{9,8},{12,9},{13,12},{2,15},{3,2},{... | collective-permute-start | bytes 3145736 | tf_op jit(solution)/shard_map/ppermute | solution.py:18
  58.5 20.1 %collective-permute-start.2 = (f32[2,256,512]{1,2,0:T(8,128)}, f32[2,256,512]{1,2,0:T(8,128)}, u32[]{:S(2)}, u32[]{:S(2)}) collective-permute-start(f32[2,256,512]{1,2,0:T(8,128)} %collective-permute-done.1), channel_id=1, source_target_pairs={{0,1},{1,4},{4,5},{5,8},{8,9},{9,12},{12,13},{13,0},{2,3},{3,6},{6... | collective-permute-start | bytes 3145736 | tf_op jit(solution)/shard_map/ppermute | solution.py:16
  60.5 46.4 %collective-permute-start.6 = (f32[2,256,512]{1,2,0:T(8,128)}, f32[2,256,512]{1,2,0:T(8,128)}, u32[]{:S(2)}, u32[]{:S(2)}) collective-permute-start(f32[2,256,512]{1,2,0:T(8,128)} %collective-permute-done.5), channel_id=1, source_target_pairs={{0,13},{1,0},{4,1},{5,4},{8,5},{9,8},{12,9},{13,12},{2,15},{3,2},{... | collective-permute-start | bytes 3145736 | tf_op jit(solution)/shard_map/ppermute | solution.py:18
  78.7 18.7 %collective-permute-start.3 = (f32[2,256,512]{1,2,0:T(8,128)}, f32[2,256,512]{1,2,0:T(8,128)}, u32[]{:S(2)}, u32[]{:S(2)}) collective-permute-start(f32[2,256,512]{1,2,0:T(8,128)} %collective-permute-done.2), channel_id=1, source_target_pairs={{0,1},{1,4},{4,5},{5,8},{8,9},{9,12},{12,13},{13,0},{2,3},{3,6},{6... | collective-permute-start | bytes 3145736 | tf_op jit(solution)/shard_map/ppermute | solution.py:16
  80.9 31.4 %copy-start.6 = (f32[2,256,512]{1,2,0:T(8,128)S(1)}, f32[2,256,512]{1,2,0:T(8,128)}, u32[]{:S(2)}) copy-start(f32[2,256,512]{1,2,0:T(8,128)} %copy-done.5) | copy-start | bytes 3145732
  80.9 31.6 %copy-start.2 = (f32[256,512]{0,1:T(8,128)S(1)}, f32[256,512]{0,1:T(8,128)}, u32[]{:S(2)}) copy-start(f32[256,512]{0,1:T(8,128)} %copy-done.1) | copy-start | bytes 1572868
  80.9 31.6 %copy-start.4 = (f32[256,512]{0,1:T(8,128)S(1)}, f32[256,512]{0,1:T(8,128)}, u32[]{:S(2)}) copy-start(f32[256,512]{0,1:T(8,128)} %copy-done.3) | copy-start | bytes 1572868
  116.7 12.6 %copy-start.7 = (s32[128]{0:T(128)S(1)}, s32[128]{0:T(128)}, u32[]{:S(2)}) copy-start(s32[128]{0:T(128)} %param.9) | copy-start | bytes 1540
  450.8 1.0 copy-start
Sparse Core Ops, SparseCore 0:
  451.9 26.8 reduce-scatter.1
